TPU v7x, 256 devices: a whole 4x4x8 slice. The times are simulated.
256 devices in a mesh: seq: 64 (over y, z, core), tr: 2 (over x_lo), tc: 2 (over x_hi).
Axes of the slice: x: 4 (x_hi: 2, x_lo: 2; x = x_hi * 2 + x_lo), y: 4, z: 8, core: 2. Of those that a mesh axis runs over, the one named last changes fastest.
Arguments:
- activations: bfloat16 [65536, 1024], P('seq', ('tr', 'tc')), may hold values from -6 to 6
- seg_len: int32 [64], P('seq'), may hold values from 1 to 1024, as said below
- seg_start: int32 [64], P('seq'), may hold values from 0 to 1, as said below
- memory_rates: float32 [3, 64, 8], P(None, 'seq'), may hold values from 0 to 1, as said below
- w_qkv: bfloat16 [1024, 3, 1024], P(None, None, ('tr', 'tc')), may hold values from -0.1875 to 0.1875
- conv_w: float32 [4, 3, 1024], P(None, None, ('tr', 'tc')), may hold values from -3 to 3
- persistent: bfloat16 [2, 16, 1024], P(None, None, ('tr', 'tc')), may hold values from -6 to 6
- w_out: bfloat16 [1024, 1024], P(('tr', 'tc')), may hold values from -0.1875 to 0.1875
- w_gate: bfloat16 [1024, 2816], P(None, ('tr', 'tc')), may hold values from -0.1875 to 0.1875
- w_up: bfloat16 [1024, 2816], P(None, ('tr', 'tc')), may hold values from -0.1875 to 0.1875
- w_down: bfloat16 [2816, 1024], P(('tr', 'tc')), may hold values from -0.109375 to 0.109375
Outputs:
- layer_out: bfloat16 [65536, 1024], P('seq', ('tr', 'tc'))
Inputs may be any that keep to these rules, and one draw needn't show every extreme that they name: `seg_start`: 1 where a segment begins a prompt, 0 where it continues the prompt of the segment before; segment 0 begins a prompt; a prompt spans at most 32 segments, and in every draw one prompt spans exactly that many. `seg_len`: live tokens at the head of each segment; every segment of a prompt but its last is full. `memory_rates`: all three tables lie strictly between 0 and 1.
All inputs are finite; a program needn't handle non-finite values.
Results may differ from a plain program's by a relative error of at most 0.015.
Values may be sent and summed in bfloat16 or wider, within the bound.
No kernel may reach another device: no remote copies, remote signals or barrier semaphores. Data moves between devices by JAX's collectives and lax.ppermute only.
A program may use at most 192 MiB of HBM per device.

v0:
```python
import jax
import jax.numpy as jnp
from jax import lax
from jax.sharding import PartitionSpec as P

HD = 128
SEG = 1024
CONV = 4
epsilon = 1e-06
score_scale = 8.0


def passed_along(block, axis, distance):
    devices = range(lax.axis_size(axis))
    route = [(i - distance, i) for i in devices if i - distance in devices]
    return lax.ppermute(block, axis, route)


def carried_in(array, axis, combine, identity):
    count, index = (lax.axis_size(axis), lax.axis_index(axis))
    everything = jax.tree.map(
        lambda part, kind: lax.all_gather(part.astype(kind), axis),
        array,
        (jnp.bfloat16, jnp.bfloat16),
    )
    start = jax.tree.map(
        lambda part, zero: jnp.broadcast_to(jnp.asarray(zero, part.dtype), part.shape),
        array,
        identity,
    )

    def step(k, before):
        reached = k < index
        new = combine(
            before, jax.tree.map(lambda part, own: part[k].astype(own.dtype), everything, array)
        )
        return jax.tree.map(lambda a, b: jnp.where(reached, a, b), new, before)

    return lax.fori_loop(0, count, step, start)


def unit_rows(values_in):
    return values_in * lax.rsqrt(jnp.sum(values_in * values_in, -1, keepdims=True) + epsilon)


def exact_product(left, right):
    return jnp.matmul(left, right, precision=lax.Precision.HIGHEST)


def combine(earlier, later):
    return (exact_product(later[0], earlier[0]), exact_product(later[0], earlier[1]) + later[1])


def body(
    activations,
    seg_len,
    seg_start,
    memory_rates,
    w_qkv,
    conv_w,
    persistent,
    w_out,
    w_gate,
    w_up,
    w_down,
):
    token_rows, local_feat = activations.shape
    seg_count = seg_len.shape[0]
    full_width = w_qkv.shape[0]
    head_width = w_qkv.shape[2]
    local_heads = head_width // HD
    group_index = lax.axis_index(("tr", "tc"))
    wide = w_qkv.reshape(full_width, 3 * head_width)
    row_ids = jnp.arange(token_rows, dtype=jnp.int32)
    position = row_ids % SEG
    segment_of = row_ids // SEG
    continuing = seg_start[segment_of] == 0
    piece = lax.all_gather(activations, ("tr", "tc"), axis=1, tiled=True)
    piece_f = piece.astype(jnp.float32)
    projected = jnp.dot(piece, wide, preferred_element_type=jnp.float32)
    squares = jnp.sum(piece_f * piece_f, -1)
    qkv = (projected * lax.rsqrt(squares / full_width + epsilon)[:, None]).astype(jnp.bfloat16)
    edge_rows = passed_along(qkv[token_rows - (CONV - 1) :], "seq", 1)
    extended = jnp.concatenate([edge_rows, qkv], 0)
    taps = conv_w.reshape(CONV, 3 * head_width)
    convolved = jnp.zeros((token_rows, 3 * head_width), jnp.float32)
    for offset in range(CONV):
        shifted = extended[CONV - 1 - offset : CONV - 1 - offset + token_rows].astype(jnp.float32)
        valid = (position >= offset) | continuing
        convolved = convolved + jnp.where(valid[:, None], taps[offset] * shifted, 0.0)
    parts = convolved.reshape(token_rows, 3, local_heads, HD)
    query_n = unit_rows(parts[:, 0]).astype(jnp.bfloat16)
    key_n = unit_rows(parts[:, 1]).astype(jnp.bfloat16)
    value_n = parts[:, 2].astype(jnp.bfloat16)
    pkeys = unit_rows(persistent[0].astype(jnp.float32).reshape(-1, local_heads, HD)).astype(
        jnp.bfloat16
    )
    pvalues = persistent[1].reshape(-1, local_heads, HD)
    persist_rows = pkeys.shape[0]
    live = position < seg_len[segment_of]
    keys_live = jnp.where(live[:, None, None], key_n, jnp.zeros((), jnp.bfloat16)).reshape(
        seg_count, SEG, local_heads, HD
    )
    value_segs = value_n.reshape(seg_count, SEG, local_heads, HD)
    a_mats = jnp.einsum("cthi,cthj->chij", keys_live, keys_live, preferred_element_type=jnp.float32)
    b_mats = jnp.einsum(
        "cthi,cthj->chij", keys_live, value_segs, preferred_element_type=jnp.float32
    )
    my_rates = lax.dynamic_slice_in_dim(memory_rates, group_index * local_heads, local_heads, 2)
    decay_factor = my_rates[0][:, :, None, None]
    eta = my_rates[1][:, :, None, None]
    theta = my_rates[2][:, :, None, None]
    keep = (1 - seg_start).astype(jnp.float32)[:, None, None, None]
    identity = jnp.eye(HD, dtype=jnp.float32)
    upper = jnp.concatenate([(1.0 - decay_factor) * identity - theta * a_mats, eta * identity], -1)
    lower = jnp.concatenate([-theta * a_mats, eta * identity], -1)
    seg_maps = jnp.concatenate([upper, lower], -2) * keep
    seg_shifts = jnp.concatenate([theta * b_mats, theta * b_mats], -2)
    dev_map = seg_maps[0]
    dev_shift = seg_shifts[0]
    neutral = (
        jnp.broadcast_to(jnp.eye(2 * HD, dtype=jnp.float32), dev_map.shape),
        jnp.zeros_like(dev_shift),
    )
    _, state = carried_in((dev_map, dev_shift), "seq", combine, neutral)
    seg_index = 0
    memory_in = state[:, :HD] * keep[seg_index]
    query_seg = query_n.astype(jnp.float32)
    retr_parts = jnp.einsum("thi,hij->thj", query_seg, memory_in, precision=lax.Precision.HIGHEST)
    mem = retr_parts * lax.rsqrt(jnp.mean(retr_parts * retr_parts, -1, keepdims=True) + epsilon)
    block_rows = min(512, SEG)
    attn_parts = []
    seg_index = 0
    first = seg_index * SEG
    keys_all = jnp.concatenate([pkeys, key_n], 0)
    values_all = jnp.concatenate([pvalues, value_n], 0)
    cols_k = jnp.arange(persist_rows + SEG, dtype=jnp.int32)[None, :] - persist_rows
    for block_start in range(0, SEG, block_rows):
        query_blk = query_n[first + block_start : first + block_start + block_rows]
        scores = score_scale * jnp.einsum(
            "qhd,khd->hqk", query_blk, keys_all, preferred_element_type=jnp.float32
        )
        rows_q = block_start + jnp.arange(block_rows, dtype=jnp.int32)[:, None]
        allow = (cols_k < 0) | (cols_k <= rows_q) & (cols_k < seg_len[seg_index])
        weights = jnp.where(allow[None], jnp.exp(scores), 0.0)
        probs = (weights / jnp.sum(weights, -1, keepdims=True)).astype(jnp.bfloat16)
        attn_parts.append(
            jnp.einsum("hqk,khd->qhd", probs, values_all, preferred_element_type=jnp.float32)
        )
    attn = jnp.concatenate(attn_parts, 0)
    heads_out = (attn + mem).astype(jnp.bfloat16).reshape(token_rows, head_width)
    partial_value = jnp.dot(heads_out, w_out, preferred_element_type=jnp.float32)
    share = lax.psum_scatter(
        partial_value.astype(jnp.bfloat16), ("tr", "tc"), scatter_dimension=1, tiled=True
    ).astype(jnp.float32)
    resid = (activations.astype(jnp.float32) + share).astype(jnp.bfloat16)
    piece = lax.all_gather(resid, ("tr", "tc"), axis=1, tiled=True)
    piece_f = piece.astype(jnp.float32)
    gate = jnp.dot(piece, w_gate, preferred_element_type=jnp.float32)
    up_proj = jnp.dot(piece, w_up, preferred_element_type=jnp.float32)
    squares2 = jnp.sum(piece_f * piece_f, -1)
    inv_rms2 = lax.rsqrt(squares2 / full_width + epsilon)[:, None]
    hidden = (jax.nn.silu(gate * inv_rms2) * (up_proj * inv_rms2)).astype(jnp.bfloat16)
    down = jnp.dot(hidden, w_down, preferred_element_type=jnp.float32)
    ffn_share = lax.psum_scatter(
        down.astype(jnp.bfloat16), ("tr", "tc"), scatter_dimension=1, tiled=True
    ).astype(jnp.float32)
    return (resid.astype(jnp.float32) + ffn_share).astype(jnp.bfloat16)


def solution(mesh):
    return jax.shard_map(
        body,
        mesh=mesh,
        in_specs=(
            P("seq", ("tr", "tc")),
            P("seq"),
            P("seq"),
            P(None, "seq", None),
            P(None, None, ("tr", "tc")),
            P(None, None, ("tr", "tc")),
            P(None, None, ("tr", "tc")),
            P(("tr", "tc"), None),
            P(None, ("tr", "tc")),
            P(None, ("tr", "tc")),
            P(("tr", "tc"), None),
        ),
        out_specs=P("seq", ("tr", "tc")),
        check_vma=False,
    )
```

profile of v0, /device:TPU:1, one launch (start us, length us, event | category | flops | bytes accessed | tf_op | source)
XLA Modules:
  0.0 545.9 jit_solution(447343479801649792)
XLA Ops:
  8.0 2.6 copy.46
  11.4 51.8 %all-gather.5.cloned.1.call-done = bf16[1024,1024]{1,0:T(8,128)(2,1)} async-done(((bf16[1024,256]{1,0:T(8,128)(2,1)}), bf16[1024,1024]{1,0:T(8,128)(2,1)}) %all-gather.5.cloned.1.call-update) | async-done | bytes 2097168 | tf_op jit(solution)/shard_map/all_gather | solution.py:78
  63.1 2.1 multiply_reduce_fusion.1
  65.2 3.9 multiply_convert_fusion
  69.1 3.6 collective-permute-start
  73.5 3.8 select_add_fusion
  77.3 5.2 reshape.355
  82.5 1.7 fusion.62
  84.2 1.6 slice.86
  91.1 2.2 fusion.15
  94.0 3.0 fusion.11
  97.0 5.4 fusion.20
  102.4 4.0 fusion.9
  106.4 5.3 fusion.21
  111.7 64.4 %all-gather.9.cloned.1.call-done = bf16[64,2,256,128]{3,2,1,0:T(8,128)(2,1)} async-done(((bf16[1,2,256,128]{3,2,1,0:T(8,128)(2,1)}), bf16[64,2,256,128]{3,2,1,0:T(8,128)(2,1)}) %all-gather.9.cloned.1.call-update) | async-done | bytes 8388624 | tf_op jit(solution)/shard_map/all_gather | solution.py:22
  176.1 98.8 %all-gather.7.cloned.1.call-done = bf16[64,2,256,256]{3,2,1,0:T(8,128)(2,1)} async-done(((bf16[1,2,256,256]{3,2,1,0:T(8,128)(2,1)}), bf16[64,2,256,256]{3,2,1,0:T(8,128)(2,1)}) %all-gather.7.cloned.1.call-update) | async-done | bytes 16777232 | tf_op jit(solution)/shard_map/all_gather | solution.py:22
  274.9 92.7 %while.14 = (s32[]{:T(128)}, f32[2,256,128]{2,1,0:T(8,128)S(1)}, s32[]{:T(128)}, bf16[64,2,256,256]{3,2,1,0:T(8,128)(2,1)}, bf16[64,2,256,128]{3,2,1,0:T(8,128)(2,1)}, /*index=5*/s32[]{:T(128)}, s32[]{:T(128)}) while((s32[]{:T(128)}, f32[2,256,128]{2,1,0:T(8,128)S(1)}, s32[]{:T(128)}, bf16[64,2,256,256]{3,2,1,0:T(8,128)(2,1)}, ...), condition=%wide.region_7.8_spmd.clone, body=%wide.region_6.7_spmd.clone.sunk | while | flops 201654272 | bytes 1706599 | solution.py:39
  275.0 1.4 fusion.83
  279.4 1.4 fusion.83
  280.8 1.4 fusion.83
  282.2 1.4 fusion.83
  283.7 1.4 fusion.83
  285.1 1.4 fusion.83
  286.6 1.4 fusion.83
  288.0 1.4 fusion.83
  289.5 1.4 fusion.83
  290.9 1.4 fusion.83
  292.4 1.4 fusion.83
  293.8 1.4 fusion.83
  295.3 1.4 fusion.83
  296.7 1.4 fusion.83
  298.2 1.4 fusion.83
  299.6 1.4 fusion.83
  301.1 1.4 fusion.83
  302.5 1.4 fusion.83
  304.0 1.4 fusion.83
  305.4 1.4 fusion.83
  306.9 1.4 fusion.83
  308.3 1.4 fusion.83
  369.7 3.2 convolution_convert_fusion
  373.0 45.7 %reduce-scatter.3.cloned.1.call-done = bf16[1024,256]{1,0:T(8,128)(2,1)} async-done(((bf16[1024,1024]{1,0:T(8,128)(2,1)}), bf16[1024,256]{1,0:T(8,128)(2,1)}) %reduce-scatter.3.cloned.1.call-update) | async-done | bytes 524304 | tf_op jit(solution)/shard_map/reduce_scatter | solution.py:153
  418.7 2.0 add_convert_fusion.1
  421.0 50.0 %all-gather.11.cloned.1.call-done = bf16[1024,1024]{1,0:T(8,128)(2,1)} async-done(((bf16[1024,256]{1,0:T(8,128)(2,1)}), bf16[1024,1024]{1,0:T(8,128)(2,1)}) %all-gather.11.cloned.1.call-update) | async-done | bytes 2097168 | tf_op jit(solution)/shard_map/all_gather | solution.py:157
  471.0 2.1 multiply_reduce_fusion
  473.1 4.9 fusion.64
  478.0 7.8 %convolution_convert_fusion.1 = bf16[1024,1024]{1,0:T(8,128)(2,1)} fusion(bf16[704,1024]{1,0:T(8,128)(2,1)S(1)} %copy-done, f32[1024,704]{0,1:T(8,128)} %fusion.64, bf16[1024,1024]{1,0:T(8,128)(2,1)} %all-gather.11.cloned.1.call-done, bf16[1024,704]{0,1:T(8,128)(2,1)} %param.22, f32[1024]{0:T(1024)S(1)} %add_rsqrt_fusion.3), kind=kOutput, calls=%fused_computation.31 | convolution fusion | flops 2959605760 | bytes 9965568 | tf_op jit(solution)/shard_map/dot_general | solution.py:164
  485.8 51.2 %reduce-scatter.5.cloned.1.call-done = bf16[1024,256]{1,0:T(8,128)(2,1)} async-done(((bf16[1024,1024]{1,0:T(8,128)(2,1)}), bf16[1024,256]{1,0:T(8,128)(2,1)}) %reduce-scatter.5.cloned.1.call-update) | async-done | bytes 524304 | tf_op jit(solution)/shard_map/reduce_scatter | solution.py:165
  537.1 2.0 add_convert_fusion
  (187 shorter events, 69.4 us)
Async XLA Ops:
  6.5 471.5 %copy-start = (bf16[704,1024]{1,0:T(8,128)(2,1)S(1)}, bf16[704,1024]{1,0:T(8,128)(2,1)}, u32[]{:S(2)}) copy-start(bf16[704,1024]{1,0:T(8,128)(2,1)} %param.23) | copy-start | bytes 4325380
  6.5 4.8 copy-start.9
  6.5 56.6 %all-gather.5.cloned.1.call-start = ((), (), s32[]{:S(2)}) async-start(), calls=%async_computation.2 | async-start | bytes 2621440 | tf_op jit(solution)/shard_map/all_gather | solution.py:78
  7.3 168.8 %all-gather.9.cloned.1.call-start = ((), (), s32[]{:S(2)}) async-start(), calls=%async_computation.4 | async-start | bytes 8519680 | tf_op jit(solution)/shard_map/all_gather | solution.py:22
  65.2 7.5 %copy-start.10 = (f32[3,1,8]{2,1,0:T(1,128)S(1)}, f32[3,1,8]{2,1,0:T(1,128)}, u32[]{:S(2)}) copy-start(f32[3,1,8]{2,1,0:T(1,128)} %param.16) | copy-start | bytes 292
  69.1 4.4 collective-permute-start
  86.5 3.1 copy-start.4
  86.5 4.3 copy-start.8
  86.6 0.9 copy-start.7
  88.8 186.2 %all-gather.7.cloned.1.call-start = ((), (), s32[]{:S(2)}) async-start(), calls=%async_computation.3 | async-start | bytes 17039360 | tf_op jit(solution)/shard_map/all_gather | solution.py:22
  90.5 328.2 %reduce-scatter.3.cloned.1.call-start = ((), (), s32[]{:S(2)}) async-start(), calls=%async_computation.5 | async-start | bytes 2621440 | tf_op jit(solution)/shard_map/reduce_scatter | solution.py:153
  91.0 3.0 copy-start.5
  97.0 5.4 copy-start.3
  274.9 93.5 %copy-start.6 = (f32[512,2,128]{0,2,1:T(8,128)S(1)}, f32[512,2,128]{0,2,1:T(8,128)}, u32[]{:S(2)}) copy-start(f32[512,2,128]{0,2,1:T(8,128)} %fusion.20) | copy-start | bytes 1572868
  369.7 49.0 %copy-start.2 = (bf16[1024,256]{1,0:T(8,128)(2,1)S(1)}, bf16[1024,256]{1,0:T(8,128)(2,1)}, u32[]{:S(2)}) copy-start(bf16[1024,256]{1,0:T(8,128)(2,1)} %param.13) | copy-start | bytes 1572868
  372.9 100.2 %copy-start.11 = (bf16[1024,704]{0,1:T(8,128)(2,1)S(1)}, bf16[1024,704]{0,1:T(8,128)(2,1)}, u32[]{:S(2)}) copy-start(bf16[1024,704]{0,1:T(8,128)(2,1)} %param.21) | copy-start | bytes 4325380
  372.9 98.1 %all-gather.11.cloned.1.call-start = ((), (), s32[]{:S(2)}) async-start(), calls=%async_computation.6 | async-start | bytes 2621440 | tf_op jit(solution)/shard_map/all_gather | solution.py:157
  420.7 116.4 %reduce-scatter.5.cloned.1.call-start = ((), (), s32[]{:S(2)}) async-start(), calls=%async_computation.7 | async-start | bytes 2621440 | tf_op jit(solution)/shard_map/reduce_scatter | solution.py:165
  478.0 59.1 %copy-start.1 = (bf16[1024,256]{1,0:T(8,128)(2,1)S(1)}, bf16[1024,256]{1,0:T(8,128)(2,1)}, u32[]{:S(2)}) copy-start(bf16[1024,256]{1,0:T(8,128)(2,1)} %add_convert_fusion.1) | copy-start | bytes 1572868
Sparse Core Ops, SparseCore 0:
  9.1 53.9 all-gather.4
  88.9 87.1 all-gather.8
  178.9 96.0 all-gather.6
  373.1 45.6 reduce-scatter.2
  420.8 50.1 all-gather.10
  486.0 51.0 reduce-scatter.4
where the time goes:
time: 548 us; the launch traced here: 546 us
  waiting for transfers between devices  363 us (66%)
  matrix products  128 us (23%)
  other arithmetic  17.2 us (3%)
  local copies, waits for them, and re-layouts  15.2 us (3%)
  between operations  15.1 us (3%)
    all_gather x2, waiting for transfers between devices, carried_in(): lax.all_gather(part.astype(kind), axis)  163 us
    dot_general x64, matrix products, exact_product(): return jnp.matmul(left, right, precision=lax.Precision.HIGHEST)  89 us
    all_gather x1, waiting for transfers between devices, body(): piece = lax.all_gather(activations, ('tr', 'tc'), axis=1, tiled=True)  51.8 us
    reduce_scatter x1, waiting for transfers between devices, body(): lax.psum_scatter(down.astype(jnp.bfloat16), ('tr', 'tc'), scatter_dimensi...  51.2 us
    all_gather x1, waiting for transfers between devices, body(): piece = lax.all_gather(resid, ('tr', 'tc'), axis=1, tiled=True)  50 us
    reduce_scatter x1, waiting for transfers between devices, body(): lax.psum_scatter(partial_value.astype(jnp.bfloat16), ('tr', 'tc'), scatte...  45.7 us
  transfers between devices with their start and end apart: 7, of which 7 were waited for; matrix products, arithmetic and copies ran while one was open for 5% of the time, Pallas kernels for 0%

commit v1 on v0

--- a/solution.py
+++ b/solution.py
@@ -154,7 +154,9 @@
         partial_value.astype(jnp.bfloat16), ("tr", "tc"), scatter_dimension=1, tiled=True
     ).astype(jnp.float32)
     resid = (activations.astype(jnp.float32) + share).astype(jnp.bfloat16)
-    piece = lax.all_gather(resid, ("tr", "tc"), axis=1, tiled=True)
+    piece = jnp.concatenate(
+        lax.all_to_all(jnp.stack([resid] * lax.axis_size(("tr", "tc"))), ("tr", "tc"), 0, 0), axis=1
+    )
     piece_f = piece.astype(jnp.float32)
     gate = jnp.dot(piece, w_gate, preferred_element_type=jnp.float32)
     up_proj = jnp.dot(piece, w_up, preferred_element_type=jnp.float32)

time: 548 us -> 520 us (0.949)
  waiting for transfers between devices: 363 us -> 312 us
  blocking collectives: 0 us -> 27.7 us
    all_gather x1 -> x0, waiting for transfers between devices: 50 us -> none  [body(): piece = lax.all_gather(resid, ('tr', 'tc'), axis=1, tiled=True)]
    all_to_all x0 -> x1, blocking collectives: none -> 27.7 us  [body(): lax.all_to_all(jnp.stack([resid] * lax.axis_size(('tr', 'tc'))), ('tr', '...]
  transfers between devices with their start and end apart: 7 -> 6, of which waited for: 7 -> 6; matrix products, arithmetic and copies ran while one was open for 5% -> 5% of each run, Pallas kernels for 0% -> 0%
where the time goes in v1:
time: 520 us; the launch traced here: 518 us
  waiting for transfers between devices  312 us (60%)
  matrix products  126 us (24%)
  blocking collectives  27.7 us (5%)
  local copies, waits for them, and re-layouts  16.3 us (3%)
  other arithmetic  15 us (3%)
  between operations  14.8 us (3%)
    all_gather x2, waiting for transfers between devices, carried_in(): lax.all_gather(part.astype(kind), axis)  163 us
    dot_general x64, matrix products, exact_product(): return jnp.matmul(left, right, precision=lax.Precision.HIGHEST)  89 us
    all_gather x1, waiting for transfers between devices, body(): piece = lax.all_gather(activations, ('tr', 'tc'), axis=1, tiled=True)  51.8 us
    reduce_scatter x1, waiting for transfers between devices, body(): lax.psum_scatter(down.astype(jnp.bfloat16), ('tr', 'tc'), scatter_dimensi...  50.2 us
    reduce_scatter x1, waiting for transfers between devices, body(): lax.psum_scatter(partial_value.astype(jnp.bfloat16), ('tr', 'tc'), scatte...  45.7 us
    all_to_all x1, blocking collectives, body(): lax.all_to_all(jnp.stack([resid] * lax.axis_size(('tr', 'tc'))), ('tr', '...  27.7 us
    dot_general x2, matrix products, body(): jnp.einsum('hqk,khd->qhd', probs, values_all, preferred_element_type=jnp....  10.7 us
  transfers between devices with their start and end apart: 6, of which 6 were waited for; matrix products, arithmetic and copies ran while one was open for 5% of the time, Pallas kernels for 0%

profile of v1, /device:TPU:1, one launch (start us, length us, event | category | flops | bytes accessed | tf_op | source)
XLA Modules:
  0.0 518.5 jit_solution(12935928732768936879)
XLA Ops:
  8.0 2.6 copy.48
  11.3 51.8 %all-gather.4.cloned.1.call-done = bf16[1024,1024]{1,0:T(8,128)(2,1)} async-done(((bf16[1024,256]{1,0:T(8,128)(2,1)}), bf16[1024,1024]{1,0:T(8,128)(2,1)}) %all-gather.4.cloned.1.call-update) | async-done | bytes 2097168 | tf_op jit(solution)/shard_map/all_gather | solution.py:78
  63.1 2.1 multiply_reduce_fusion.1
  65.2 3.9 multiply_convert_fusion
  69.1 3.6 collective-permute-start
  73.5 3.8 select_add_fusion
  77.3 5.2 %reshape.363 = f32[1024,3,2,128]{3,2,1,0:T(2,128)} reshape(f32[1024,768]{1,0:T(8,128)} %select_add_fusion) | data formatting | bytes 6291456 | tf_op jit(solution)/shard_map/reshape | solution.py:91
  82.5 1.7 fusion.62
  84.2 1.6 slice.86
  91.2 2.2 fusion.15
  94.1 3.0 fusion.11
  97.0 5.4 %fusion.20 = f32[512,2,128]{0,2,1:T(8,128)} fusion(f32[2,512,1040]{1,2,0:T(8,128)} %fusion.11, bf16[1024,2,128]{2,0,1:T(8,128)(2,1)} %bitcast.73, bf16[16,2,128]{2,0,1:T(8,128)(2,1)S(1)} %copy.50), kind=kOutput, calls=%fused_computation.38 | convolution fusion | flops 275826688 | bytes 5316608 | tf_op jit(solution)/shard_map/hqk,khd->qhd/dot_general | solution.py:148
  102.4 4.0 fusion.9
  106.4 5.3 %fusion.21 = f32[512,2,128]{0,2,1:T(8,128)} fusion(f32[2,512,1040]{1,2,0:T(8,128)} %fusion.9, bf16[1024,2,128]{2,0,1:T(8,128)(2,1)} %bitcast.74, bf16[16,2,128]{2,0,1:T(8,128)(2,1)S(1)} %copy.50), kind=kOutput, calls=%fused_computation.39 | convolution fusion | flops 275826688 | bytes 5316608 | tf_op jit(solution)/shard_map/hqk,khd->qhd/dot_general | solution.py:148
  111.7 64.4 %all-gather.8.cloned.1.call-done = bf16[64,2,256,128]{3,2,1,0:T(8,128)(2,1)} async-done(((bf16[1,2,256,128]{3,2,1,0:T(8,128)(2,1)}), bf16[64,2,256,128]{3,2,1,0:T(8,128)(2,1)}) %all-gather.8.cloned.1.call-update) | async-done | bytes 8388624 | tf_op jit(solution)/shard_map/all_gather | solution.py:22
  176.1 98.9 %all-gather.6.cloned.1.call-done = bf16[64,2,256,256]{3,2,1,0:T(8,128)(2,1)} async-done(((bf16[1,2,256,256]{3,2,1,0:T(8,128)(2,1)}), bf16[64,2,256,256]{3,2,1,0:T(8,128)(2,1)}) %all-gather.6.cloned.1.call-update) | async-done | bytes 16777232 | tf_op jit(solution)/shard_map/all_gather | solution.py:22
  275.0 92.7 %while.14 = (s32[]{:T(128)}, f32[2,256,128]{2,1,0:T(8,128)S(1)}, s32[]{:T(128)}, bf16[64,2,256,256]{3,2,1,0:T(8,128)(2,1)}, bf16[64,2,256,128]{3,2,1,0:T(8,128)(2,1)}, /*index=5*/s32[]{:T(128)}, s32[]{:T(128)}) while((s32[]{:T(128)}, f32[2,256,128]{2,1,0:T(8,128)S(1)}, s32[]{:T(128)}, bf16[64,2,256,256]{3,2,1,0:T(8,128)(2,1)}, ...), condition=%wide.region_7.8_spmd.clone, body=%wide.region_6.7_spmd.clone.sunk | while | flops 201654272 | bytes 1706599 | solution.py:39
  275.0 1.4 fusion.83
  276.5 1.4 fusion.83
  278.0 1.4 fusion.83
  279.4 1.4 fusion.83
  280.9 1.4 fusion.83
  282.3 1.4 fusion.83
  283.8 1.4 fusion.83
  285.2 1.4 fusion.83
  286.7 1.4 fusion.83
  288.1 1.4 fusion.83
  289.6 1.4 fusion.83
  291.0 1.4 fusion.83
  292.5 1.4 fusion.83
  293.9 1.4 fusion.83
  295.4 1.4 fusion.83
  296.8 1.4 fusion.83
  298.2 1.4 fusion.83
  299.7 1.4 fusion.83
  301.1 1.4 fusion.83
  302.6 1.4 fusion.83
  304.0 1.4 fusion.83
  305.5 1.4 fusion.83
  306.9 1.4 fusion.83
  308.4 1.4 fusion.83
  369.8 3.2 convolution_convert_fusion
  373.1 45.7 %reduce-scatter.3.cloned.1.call-done = bf16[1024,256]{1,0:T(8,128)(2,1)} async-done(((bf16[1024,1024]{1,0:T(8,128)(2,1)}), bf16[1024,256]{1,0:T(8,128)(2,1)}) %reduce-scatter.3.cloned.1.call-update) | async-done | bytes 524304 | tf_op jit(solution)/shard_map/reduce_scatter | solution.py:153
  421.1 27.7 %all_to_all.5 = bf16[4,1024,256]{1,2,0:T(8,128)(2,1)S(1)} all-to-all(bf16[4,1024,256]{1,2,0:T(8,128)(2,1)S(1)} %stack.2), channel_id=1, replica_groups=mesh['seq'=64,'tr'=2,'tc'=2] {'tr','tc'}, dimensions={0} | all-to-all | bytes 4194304 | tf_op jit(solution)/shard_map/all_to_all | solution.py:158
  449.3 3.2 fusion.64
  452.5 7.1 %convolution_convert_fusion.1 = bf16[1024,1024]{1,0:T(8,128)(2,1)} fusion(bf16[704,1024]{1,0:T(8,128)(2,1)S(1)} %copy-done, f32[1024,704]{0,1:T(8,128)} %fusion.64, bf16[1024,704]{0,1:T(8,128)(2,1)} %param.22, bf16[1024,1024]{0,1:T(8,128)(2,1)S(1)} %bitcast.69, f32[1024]{0:T(1024)S(1)} %add_rsqrt_fusion.3), kind=kOutput, calls=%fused_computation.31 | convolution fusion | flops 2959605760 | bytes 9965568 | tf_op jit(solution)/shard_map/dot_general | solution.py:166
  459.7 50.2 %reduce-scatter.5.cloned.1.call-done = bf16[1024,256]{1,0:T(8,128)(2,1)} async-done(((bf16[1024,1024]{1,0:T(8,128)(2,1)}), bf16[1024,256]{1,0:T(8,128)(2,1)}) %reduce-scatter.5.cloned.1.call-update) | async-done | bytes 524304 | tf_op jit(solution)/shard_map/reduce_scatter | solution.py:167
  509.8 2.1 add_convert_fusion
  (187 shorter events, 69.1 us)
Async XLA Ops:
  6.5 446.0 %copy-start = (bf16[704,1024]{1,0:T(8,128)(2,1)S(1)}, bf16[704,1024]{1,0:T(8,128)(2,1)}, u32[]{:S(2)}) copy-start(bf16[704,1024]{1,0:T(8,128)(2,1)} %param.23) | copy-start | bytes 4325380
  6.5 4.7 copy-start.9
  6.5 56.6 %all-gather.4.cloned.1.call-start = ((), (), s32[]{:S(2)}) async-start(), calls=%async_computation.3 | async-start | bytes 2621440 | tf_op jit(solution)/shard_map/all_gather | solution.py:78
  7.3 168.9 %all-gather.8.cloned.1.call-start = ((), (), s32[]{:S(2)}) async-start(), calls=%async_computation.5 | async-start | bytes 8519680 | tf_op jit(solution)/shard_map/all_gather | solution.py:22
  65.2 7.6 %copy-start.10 = (f32[3,1,8]{2,1,0:T(1,128)S(1)}, f32[3,1,8]{2,1,0:T(1,128)}, u32[]{:S(2)}) copy-start(f32[3,1,8]{2,1,0:T(1,128)} %param.16) | copy-start | bytes 292
  69.1 4.4 collective-permute-start
  86.5 3.2 copy-start.4
  86.5 4.3 copy-start.8
  86.6 0.9 copy-start.7
  88.8 186.2 %all-gather.6.cloned.1.call-start = ((), (), s32[]{:S(2)}) async-start(), calls=%async_computation.4 | async-start | bytes 17039360 | tf_op jit(solution)/shard_map/all_gather | solution.py:22
  90.6 328.2 %reduce-scatter.3.cloned.1.call-start = ((), (), s32[]{:S(2)}) async-start(), calls=%async_computation.6 | async-start | bytes 2621440 | tf_op jit(solution)/shard_map/reduce_scatter | solution.py:153
  91.1 3.0 copy-start.5
  97.0 5.4 %copy-start.3 = (pred[512,1040]{0,1:T(8,128)(4,1)S(1)}, pred[512,1040]{0,1:T(8,128)(4,1)}, u32[]{:S(2)}) copy-start(pred[512,1040]{0,1:T(8,128)(4,1)} %get-tuple-element.150) | copy-start | bytes 1597444
  275.0 93.5 %copy-start.6 = (f32[512,2,128]{0,2,1:T(8,128)S(1)}, f32[512,2,128]{0,2,1:T(8,128)}, u32[]{:S(2)}) copy-start(f32[512,2,128]{0,2,1:T(8,128)} %fusion.20) | copy-start | bytes 1572868
  369.8 49.0 %copy-start.2 = (bf16[1024,256]{1,0:T(8,128)(2,1)S(1)}, bf16[1024,256]{1,0:T(8,128)(2,1)}, u32[]{:S(2)}) copy-start(bf16[1024,256]{1,0:T(8,128)(2,1)} %param.13) | copy-start | bytes 1572868
  373.0 136.8 %reduce-scatter.5.cloned.1.call-start = ((), (), s32[]{:S(2)}) async-start(), calls=%async_computation.7 | async-start | bytes 2621440 | tf_op jit(solution)/shard_map/reduce_scatter | solution.py:167
  420.0 0.8 copy-start.1
  421.1 28.2 %copy-start.11 = (bf16[1024,704]{0,1:T(8,128)(2,1)S(1)}, bf16[1024,704]{0,1:T(8,128)(2,1)}, u32[]{:S(2)}) copy-start(bf16[1024,704]{0,1:T(8,128)(2,1)} %param.21) | copy-start | bytes 4325380
Sparse Core Ops, SparseCore 0:
  9.1 53.9 all-gather.3
  88.9 87.1 all-gather.7
  178.9 96.0 all-gather.5
  373.1 45.6 reduce-scatter.2
  459.8 50.0 reduce-scatter.4
